TPU v7x, 512 devices: a whole 4x4x16 slice. The times are simulated.
512 devices in a mesh: gx: 64 (over z, y), gy: 8 (over x, core).
Axes of the slice: x: 4, y: 4, z: 16, core: 2. Of those that a mesh axis runs over, the one named last changes fastest.
Arguments:
- rhs: float32 [64, 8, 128, 128], P('gx', 'gy'), may hold values from -57 to 57
- face_rows: int32 [64, 8, 4, 128], P('gx', 'gy'), may hold values from 0 to 127
- margin_weight: float32 [64, 8, 4, 128], P('gx', 'gy'), may hold values from 0.2 to 1
- local_blocks: bfloat16 [64, 8, 1, 128, 128], P('gx', 'gy'), may hold values from -0.4 to 4.4
- subdomain_inverse: bfloat16 [64, 8, 128, 640], P('gx', 'gy'), may hold values from -0.4 to 1.8
- coarse_basis: bfloat16 [64, 8, 128, 32], P('gx', 'gy'), may hold values from -0.5 to 0.5
- coarse_inverse: bfloat16 [64, 8, 32, 16384], P('gx', 'gy'), may hold values from -0.09765625 to 0.09765625
- coarse_map: int32 [512], replicated, may hold values from 0 to 511, each once
Outputs:
- solution: float32 [64, 8, 128, 128], P('gx', 'gy')
- relative_residual: float32 [128], replicated
Inputs may be any that keep to these rules, and one draw needn't show every extreme that they name: `face_rows`: rows of the subdomain, repeats possible. `coarse_map`: every position once.
All inputs are finite; a program needn't handle non-finite values.
Results may differ from a plain program's by a relative error of at most 0.004.
Values may be sent and summed in bfloat16 or wider, within the bound.
No kernel may reach another device: no remote copies, remote signals or barrier semaphores. Data moves between devices by JAX's collectives and lax.ppermute only.
A program may use at most 64 MiB of HBM per device.

v0:
```python
import jax
import numpy as np
import jax.numpy as jnp
from jax import lax
from jax.sharding import PartitionSpec as P

EPSILON = 1e-06
KEPT_SHARE = 1.0 / 64


def neighbours(rows, axis):
    count = lax.axis_size(axis)
    up = [(i, i + 1) for i in range(count - 1)]
    down = [(i + 1, i) for i in range(count - 1)]
    return (lax.ppermute(rows[1], axis, up), lax.ppermute(rows[0], axis, down))


def exchange(packs):
    below_first, above_first = neighbours(packs[0:2], "gx")
    below_second, above_second = neighbours(packs[2:4], "gy")
    return jnp.stack([below_first, above_first, below_second, above_second], axis=0)


def allsum(value):
    value = lax.psum(value, "gy")
    for axis in ("gx",):
        count = lax.axis_size(axis)
        if count & count - 1:
            value = lax.psum(value, axis)
            continue
        step = 1
        while step < count:
            value = value + lax.ppermute(value, axis, [(i, i ^ step) for i in range(count)])
            step *= 2
    return value


GATHER_ROUNDS = (("gx", 32), ("gx", 16), ("gx", 8), ("gx", 4), ("gx", 2), ("gx", 1))


def gather_rounds(count_x, count_y):
    sizes = {"gx": count_x, "gy": count_y}
    return tuple(((axis, step) for axis, step in GATHER_ROUNDS if step < sizes[axis]))


def doubling_gather(block, rounds):
    held = block[None]
    for axis, step in rounds:
        count = lax.axis_size(axis)
        got = lax.ppermute(held, axis, [(i, i ^ step) for i in range(count)])
        upper = lax.axis_index(axis) // step % 2 == 1
        held = jnp.where(
            upper, jnp.concatenate([got, held], axis=0), jnp.concatenate([held, got], axis=0)
        )
    return lax.all_gather(held.reshape(-1, block.shape[-1]), "gy", axis=0, tiled=True)


def gathered_order(rounds, count_y):
    order = []
    for outer in range(count_y):
        for position in range(2 ** len(rounds)):
            index = {"gx": 0, "gy": outer}
            for bit, (axis, step) in enumerate(rounds):
                index[axis] += (position >> bit & 1) * step
            order.append(index["gx"] * count_y + index["gy"])
    return np.asarray(order, np.int32)


def least_squares(scale_norm, first_dot, first_norm, cross_dot, second_dot, second_norm):
    radius_one = jnp.sqrt(first_dot * first_dot + first_norm * first_norm)
    cosine_one = first_dot / radius_one
    sine_one = first_norm / radius_one
    upper_entry = cosine_one * cross_dot + sine_one * second_dot
    lower_entry = cosine_one * second_dot - sine_one * cross_dot
    radius_two = jnp.sqrt(lower_entry * lower_entry + second_norm * second_norm)
    cosine_two = lower_entry / radius_two
    sine_two = second_norm / radius_two
    weight_two = -cosine_two * sine_one * scale_norm / radius_two
    weight_one = (cosine_one * scale_norm - upper_entry * weight_two) / radius_one
    return (weight_one, weight_two, sine_one * sine_two)


def on_device(
    rhs,
    face_rows,
    margin_weight,
    local_blocks,
    subdomain_inverse,
    coarse_basis,
    coarse_inverse,
    coarse_map,
):
    right_side = rhs[0, 0]
    margin_rows = face_rows[0, 0]
    margin_weights = margin_weight[0, 0]
    local_block = local_blocks[0, 0]
    inverse_rows = subdomain_inverse[0, 0]
    basis = coarse_basis[0, 0]
    coarse_rows = coarse_inverse[0, 0]
    owned_rows = right_side.shape[0]
    system_count = right_side.shape[1]
    basis_count = basis.shape[1]
    block_rows = local_block.shape[1]
    count_x = lax.axis_size("gx")
    count_y = lax.axis_size("gy")
    rounds = gather_rounds(count_x, count_y)
    gathered_map = coarse_map[gathered_order(rounds, count_y)]
    selection = (
        gathered_map[:, None] == jnp.arange(gathered_map.shape[0], dtype=jnp.int32)[None, :]
    ).astype(jnp.bfloat16)

    def margin_of(field):
        return exchange(field[margin_rows])

    def coarse_gather(residual):
        return doubling_gather(residual, rounds)

    def precondition(rounded, margin):
        extended = jnp.concatenate([rounded, margin.reshape(-1, system_count)], axis=0)
        local_part = jnp.dot(inverse_rows, extended, preferred_element_type=jnp.float32)
        residual = lax.dot_general(
            basis, rounded, (((0,), (0,)), ((), ())), preferred_element_type=jnp.float32
        ).astype(jnp.bfloat16)
        gathered = coarse_gather(residual).reshape(selection.shape[0], -1)
        placed = lax.dot_general(
            selection, gathered, (((0,), (0,)), ((), ())), preferred_element_type=jnp.float32
        ).astype(jnp.bfloat16)
        solved = jnp.dot(
            coarse_rows, placed.reshape(-1, system_count), preferred_element_type=jnp.float32
        )
        return local_part + jnp.dot(
            basis, solved.astype(jnp.bfloat16), preferred_element_type=jnp.float32
        )

    def apply_operator(vector):
        rounded = vector.astype(jnp.bfloat16)
        own_part = jnp.einsum(
            "brc,bcn->brn",
            local_block,
            rounded.reshape(-1, block_rows, system_count),
            preferred_element_type=jnp.float32,
        ).reshape(owned_rows, system_count)
        weighted = margin_weights[:, :, None] * margin_of(rounded).astype(jnp.float32)
        coupling = (
            jnp.zeros((owned_rows, system_count), jnp.float32)
            .at[margin_rows.reshape(-1)]
            .add(weighted.reshape(-1, system_count))
        )
        return own_part - coupling

    def column_norm(vector):
        return jnp.sqrt(allsum(jnp.sum(vector * vector, axis=0)) + EPSILON)

    def guarded_norm(expanded, whole, remainder):
        kept = jnp.all(jnp.isfinite(expanded) & (expanded >= KEPT_SHARE * whole))
        return lax.cond(kept, lambda vector: jnp.sqrt(expanded + EPSILON), column_norm, remainder)

    rhs_margin = margin_of(right_side)
    scale_norm = column_norm(right_side)
    krylov_one = right_side / scale_norm
    margin_one = rhs_margin / scale_norm
    precond_one = precondition(krylov_one.astype(jnp.bfloat16), margin_one.astype(jnp.bfloat16))
    applied = apply_operator(precond_one)
    applied_margin = margin_of(applied)
    sums = allsum(
        jnp.stack(
            [
                jnp.sum(applied * krylov_one, axis=0),
                jnp.sum(applied * applied, axis=0),
                jnp.sum(krylov_one * krylov_one, axis=0),
            ]
        )
    )
    first_dot = sums[0]
    remainder = applied - first_dot * krylov_one
    expanded = sums[1] - 2.0 * first_dot * first_dot + first_dot * first_dot * sums[2]
    first_norm = guarded_norm(expanded, sums[1], remainder)
    krylov_two = remainder / first_norm
    margin_two = (applied_margin - first_dot * margin_one) / first_norm
    precond_two = precondition(krylov_two.astype(jnp.bfloat16), margin_two.astype(jnp.bfloat16))
    applied = apply_operator(precond_two)
    dots = allsum(
        jnp.stack(
            [
                jnp.sum(applied * krylov_one, axis=0),
                jnp.sum(applied * krylov_two, axis=0),
                jnp.sum(applied * applied, axis=0),
                jnp.sum(krylov_one * krylov_one, axis=0),
                jnp.sum(krylov_one * krylov_two, axis=0),
                jnp.sum(krylov_two * krylov_two, axis=0),
            ]
        )
    )
    cross_dot = dots[0]
    second_dot = dots[1]
    remainder = applied - cross_dot * krylov_one - second_dot * krylov_two
    expanded = (
        dots[2]
        - 2.0 * cross_dot * cross_dot
        - 2.0 * second_dot * second_dot
        + cross_dot * cross_dot * dots[3]
        + 2.0 * cross_dot * second_dot * dots[4]
        + second_dot * second_dot * dots[5]
    )
    second_norm = guarded_norm(expanded, dots[2], remainder)
    weight_one, weight_two, relative = least_squares(
        scale_norm, first_dot, first_norm, cross_dot, second_dot, second_norm
    )
    solution = weight_one * precond_one + weight_two * precond_two
    return (solution[None, None], relative)


def solution(mesh):
    return jax.shard_map(
        on_device,
        mesh=mesh,
        in_specs=(
            P("gx", "gy", None, None),
            P("gx", "gy", None, None),
            P("gx", "gy", None, None),
            P("gx", "gy", None, None, None),
            P("gx", "gy", None, None),
            P("gx", "gy", None, None),
            P("gx", "gy", None, None),
            P(),
        ),
        out_specs=(P("gx", "gy", None, None), P()),
        check_vma=False,
    )
```

profile of v0, /device:TPU:8, one launch (start us, length us, event | category | flops | bytes accessed | tf_op | source)
XLA Modules:
  0.0 481.7 jit_solution(6558370175424277475)
XLA Ops:
  8.2 14.6 %psum.35 = f32[128]{0:T(128)S(1)} all-reduce(f32[128]{0:T(128)S(1)} %multiply_reduce_fusion.10), channel_id=1, replica_groups=mesh['gx'=64,'gy'=8] {'gy'}, use_global_device_ids=true, to_apply=%region_1.0 | all-reduce | flops 128 | bytes 1024 | tf_op jit(solution)/shard_map/psum | solution.py:25
  22.8 5.5 %collective-permute-start.12 = (f32[128]{0:T(128)S(1)}, f32[128]{0:T(128)S(1)}, u32[]{:S(2)}, u32[]{:S(2)}) collective-permute-start(f32[128]{0:T(128)S(1)} %psum.35), channel_id=1, source_target_pairs={{0,8},{8,0},{16,24},{24,16},{32,40},{40,32},{48,56},{56,48},{64,72... | collective-permute-start | bytes 1544 | tf_op jit(solution)/shard_map/ppermute | solution.py:33
  32.5 4.3 collective-permute-done.13
  48.6 7.9 %collective-permute-start.16 = (f32[128]{0:T(128)S(1)}, f32[128]{0:T(128)S(1)}, u32[]{:S(2)}, u32[]{:S(2)}) collective-permute-start(f32[128]{0:T(128)S(1)} %add.222), channel_id=1, source_target_pairs={{0,128},{8,136},{16,144},{24,152},{32,160},{40,168},{48,176},{56,1... | collective-permute-start | bytes 1544 | tf_op jit(solution)/shard_map/ppermute | solution.py:33
  58.0 14.1 %collective-permute-start.17 = (f32[128]{0:T(128)S(1)}, f32[128]{0:T(128)S(1)}, u32[]{:S(2)}, u32[]{:S(2)}) collective-permute-start(f32[128]{0:T(128)S(1)} %add.223), channel_id=1, source_target_pairs={{0,256},{8,264},{16,272},{24,280},{32,288},{40,296},{48,304},{56,3... | collective-permute-start | bytes 1544 | tf_op jit(solution)/shard_map/ppermute | solution.py:33
  74.6 12.6 %collective-permute-start.22 = (bf16[1,32,128]{2,1,0:T(8,128)(2,1)S(1)}, bf16[1,32,128]{2,1,0:T(8,128)(2,1)S(1)}, u32[]{:S(2)}, u32[]{:S(2)}) collective-permute-start(bf16[1,32,128]{2,1,0:T(8,128)(2,1)S(1)} %fusion.2), channel_id=1, source_target_pairs={{0,256},{8,264},{16,272},{24,280},{32,288},{40,296},{48,304},{56,3... | collective-permute-start | bytes 24584 | tf_op jit(solution)/shard_map/ppermute | solution.py:50
  88.9 6.4 %collective-permute-start.23 = (bf16[2,32,128]{2,1,0:T(8,128)(2,1)S(1)}, bf16[2,32,128]{2,1,0:T(8,128)(2,1)S(1)}, u32[]{:S(2)}, u32[]{:S(2)}) collective-permute-start(bf16[2,32,128]{2,1,0:T(8,128)(2,1)S(1)} %maximum_select_fusion.10), channel_id=1, source_target_pairs={{0,128},{8,136},{16,144},{24,152},{32,160},{40,168},{48,176},{56,1... | collective-permute-start | bytes 49160 | tf_op jit(solution)/shard_map/ppermute | solution.py:50
  111.4 4.3 collective-permute-start.26
  115.7 4.1 collective-permute-done.26
  122.3 5.8 %collective-permute-done.27 = bf16[32,32,128]{2,1,0:T(8,128)(2,1)S(1)} collective-permute-done((bf16[32,32,128]{2,1,0:T(8,128)(2,1)S(1)}, bf16[32,32,128]{2,1,0:T(8,128)(2,1)S(1)}, u32[]{:S(2)}, u32[]{:S(2)}) %collective-permute-start.27) | collective-permute-done | bytes 262176 | tf_op jit(solution)/shard_map/ppermute | solution.py:50
  143.3 24.8 %all-gather.3.cloned.1.call-done = bf16[16384,128]{1,0:T(8,128)(2,1)} async-done(((bf16[2048,128]{1,0:T(8,128)(2,1)}), bf16[16384,128]{1,0:T(8,128)(2,1)}) %all-gather.3.cloned.1.call-update) | async-done | bytes 4194320 | tf_op jit(solution)/shard_map/all_gather | solution.py:55
  168.1 7.4 %reshape.132 = bf16[512,4096]{1,0:T(8,128)(2,1)} reshape(bf16[16384,128]{1,0:T(8,128)(2,1)} %all-gather.3.cloned.1.call-done) | data formatting | bytes 8388608 | tf_op jit(solution)/shard_map/reshape | solution.py:124
  175.4 6.6 %convolution_convert_fusion.1 = bf16[512,4096]{1,0:T(8,128)(2,1)} fusion(bf16[512,4096]{1,0:T(8,128)(2,1)} %reshape.132, s32[512]{0:T(512)S(1)} %gather_fusion.1), kind=kOutput, calls=%fused_computation.10 | convolution fusion | flops 2149842944 | bytes 8390656 | tf_op jit(solution)/shard_map/dot_general | solution.py:125
  182.0 7.5 %reshape.133 = bf16[16384,128]{1,0:T(8,128)(2,1)} reshape(bf16[512,4096]{1,0:T(8,128)(2,1)} %convolution_convert_fusion.1) | data formatting | bytes 8388608 | tf_op jit(solution)/shard_map/reshape | solution.py:129
  208.4 14.6 %psum.36 = f32[3,128]{1,0:T(4,128)S(1)} all-reduce(f32[3,128]{1,0:T(4,128)S(1)} %pad_maximum_fusion.4), channel_id=1, replica_groups=mesh['gx'=64,'gy'=8] {'gy'}, use_global_device_ids=true, to_apply=%region_6.7 | all-reduce | flops 384 | bytes 3072 | tf_op jit(solution)/shard_map/psum | solution.py:25
  235.4 4.1 collective-permute-start.34
  241.1 4.9 %collective-permute-start.35 = (f32[3,128]{1,0:T(4,128)S(1)}, f32[3,128]{1,0:T(4,128)S(1)}, u32[]{:S(2)}, u32[]{:S(2)}) collective-permute-start(f32[3,128]{1,0:T(4,128)S(1)} %add.239), channel_id=1, source_target_pairs={{0,64},{8,72},{16,80},{24,88},{32,96},{40,104},{48,112},{56,120},{... | collective-permute-start | bytes 4616 | tf_op jit(solution)/shard_map/ppermute | solution.py:33
  247.6 9.2 %collective-permute-start.36 = (f32[3,128]{1,0:T(4,128)S(1)}, f32[3,128]{1,0:T(4,128)S(1)}, u32[]{:S(2)}, u32[]{:S(2)}) collective-permute-start(f32[3,128]{1,0:T(4,128)S(1)} %add.240), channel_id=1, source_target_pairs={{0,128},{8,136},{16,144},{24,152},{32,160},{40,168},{48,176},{56,1... | collective-permute-start | bytes 4616 | tf_op jit(solution)/shard_map/ppermute | solution.py:33
  258.3 13.0 %collective-permute-start.37 = (f32[3,128]{1,0:T(4,128)S(1)}, f32[3,128]{1,0:T(4,128)S(1)}, u32[]{:S(2)}, u32[]{:S(2)}) collective-permute-start(f32[3,128]{1,0:T(4,128)S(1)} %add.241), channel_id=1, source_target_pairs={{0,256},{8,264},{16,272},{24,280},{32,288},{40,296},{48,304},{56,3... | collective-permute-start | bytes 4616 | tf_op jit(solution)/shard_map/ppermute | solution.py:33
  274.4 12.6 %collective-permute-start.42 = (bf16[1,32,128]{2,1,0:T(8,128)(2,1)S(1)}, bf16[1,32,128]{2,1,0:T(8,128)(2,1)S(1)}, u32[]{:S(2)}, u32[]{:S(2)}) collective-permute-start(bf16[1,32,128]{2,1,0:T(8,128)(2,1)S(1)} %fusion.3), channel_id=1, source_target_pairs={{0,256},{8,264},{16,272},{24,280},{32,288},{40,296},{48,304},{56,3... | collective-permute-start | bytes 24584 | tf_op jit(solution)/shard_map/ppermute | solution.py:50
  288.6 7.5 %collective-permute-start.43 = (bf16[2,32,128]{2,1,0:T(8,128)(2,1)S(1)}, bf16[2,32,128]{2,1,0:T(8,128)(2,1)S(1)}, u32[]{:S(2)}, u32[]{:S(2)}) collective-permute-start(bf16[2,32,128]{2,1,0:T(8,128)(2,1)S(1)} %maximum_select_fusion.11), channel_id=1, source_target_pairs={{0,128},{8,136},{16,144},{24,152},{32,160},{40,168},{48,176},{56,1... | collective-permute-start | bytes 49160 | tf_op jit(solution)/shard_map/ppermute | solution.py:50
  314.7 4.7 collective-permute-done.46
  323.4 4.3 collective-permute-done.47
  340.4 26.8 %all-gather.5.cloned.1.call-done = bf16[16384,128]{1,0:T(8,128)(2,1)} async-done(((bf16[2048,128]{1,0:T(8,128)(2,1)}), bf16[16384,128]{1,0:T(8,128)(2,1)}) %all-gather.5.cloned.1.call-update) | async-done | bytes 4194320 | tf_op jit(solution)/shard_map/all_gather | solution.py:55
  367.2 7.4 %reshape.135 = bf16[512,4096]{1,0:T(8,128)(2,1)} reshape(bf16[16384,128]{1,0:T(8,128)(2,1)} %all-gather.5.cloned.1.call-done) | data formatting | bytes 8388608 | tf_op jit(solution)/shard_map/reshape | solution.py:124
  374.6 6.6 %convolution_convert_fusion = bf16[512,4096]{1,0:T(8,128)(2,1)} fusion(bf16[512,4096]{1,0:T(8,128)(2,1)} %reshape.135, s32[512]{0:T(512)S(1)} %gather_fusion.1), kind=kOutput, calls=%fused_computation.9 | convolution fusion | flops 2149842944 | bytes 8390656 | tf_op jit(solution)/shard_map/dot_general | solution.py:125
  381.2 7.4 %reshape.136 = bf16[16384,128]{1,0:T(8,128)(2,1)} reshape(bf16[512,4096]{1,0:T(8,128)(2,1)} %convolution_convert_fusion) | data formatting | bytes 8388608 | tf_op jit(solution)/shard_map/reshape | solution.py:129
  407.4 14.6 %psum.37 = f32[6,128]{1,0:T(8,128)S(1)} all-reduce(f32[6,128]{1,0:T(8,128)S(1)} %stack.126), channel_id=1, replica_groups=mesh['gx'=64,'gy'=8] {'gy'}, use_global_device_ids=true, to_apply=%region_18.19 | all-reduce | flops 768 | bytes 6144 | tf_op jit(solution)/shard_map/psum | solution.py:25
  434.6 4.1 collective-permute-start.54
  440.2 4.9 %collective-permute-start.55 = (f32[6,128]{1,0:T(8,128)S(1)}, f32[6,128]{1,0:T(8,128)S(1)}, u32[]{:S(2)}, u32[]{:S(2)}) collective-permute-start(f32[6,128]{1,0:T(8,128)S(1)} %add.249), channel_id=1, source_target_pairs={{0,64},{8,72},{16,80},{24,88},{32,96},{40,104},{48,112},{56,120},{... | collective-permute-start | bytes 9224 | tf_op jit(solution)/shard_map/ppermute | solution.py:33
  446.7 9.2 %collective-permute-start.56 = (f32[6,128]{1,0:T(8,128)S(1)}, f32[6,128]{1,0:T(8,128)S(1)}, u32[]{:S(2)}, u32[]{:S(2)}) collective-permute-start(f32[6,128]{1,0:T(8,128)S(1)} %add.250), channel_id=1, source_target_pairs={{0,128},{8,136},{16,144},{24,152},{32,160},{40,168},{48,176},{56,1... | collective-permute-start | bytes 9224 | tf_op jit(solution)/shard_map/ppermute | solution.py:33
  457.5 13.0 %collective-permute-start.57 = (f32[6,128]{1,0:T(8,128)S(1)}, f32[6,128]{1,0:T(8,128)S(1)}, u32[]{:S(2)}, u32[]{:S(2)}) collective-permute-start(f32[6,128]{1,0:T(8,128)S(1)} %add.251), channel_id=1, source_target_pairs={{0,256},{8,264},{16,272},{24,280},{32,288},{40,296},{48,304},{56,3... | collective-permute-start | bytes 9224 | tf_op jit(solution)/shard_map/ppermute | solution.py:33
  (173 shorter events, 170.4 us)
Async XLA Ops:
  7.2 160.9 %all-gather.3.cloned.1.call-start = ((), (), s32[]{:S(2)}) async-start(), calls=%async_computation | async-start | bytes 4718592 | tf_op jit(solution)/shard_map/all_gather | solution.py:55
  22.8 7.0 %collective-permute-start.12 = (f32[128]{0:T(128)S(1)}, f32[128]{0:T(128)S(1)}, u32[]{:S(2)}, u32[]{:S(2)}) collective-permute-start(f32[128]{0:T(128)S(1)} %psum.35), channel_id=1, source_target_pairs={{0,8},{8,0},{16,24},{24,16},{32,40},{40,32},{48,56},{56,48},{64,72... | collective-permute-start | bytes 1544 | tf_op jit(solution)/shard_map/ppermute | solution.py:33
  29.9 7.0 %collective-permute-start.13 = (f32[128]{0:T(128)S(1)}, f32[128]{0:T(128)S(1)}, u32[]{:S(2)}, u32[]{:S(2)}) collective-permute-start(f32[128]{0:T(128)S(1)} %add.219), channel_id=1, source_target_pairs={{0,16},{8,24},{16,0},{24,8},{32,48},{40,56},{48,32},{56,40},{64,80... | collective-permute-start | bytes 1544 | tf_op jit(solution)/shard_map/ppermute | solution.py:33
  42.3 6.3 %collective-permute-start.15 = (f32[128]{0:T(128)S(1)}, f32[128]{0:T(128)S(1)}, u32[]{:S(2)}, u32[]{:S(2)}) collective-permute-start(f32[128]{0:T(128)S(1)} %add.221), channel_id=1, source_target_pairs={{0,64},{8,72},{16,80},{24,88},{32,96},{40,104},{48,112},{56,120},{... | collective-permute-start | bytes 1544 | tf_op jit(solution)/shard_map/ppermute | solution.py:33
  48.6 9.4 %collective-permute-start.16 = (f32[128]{0:T(128)S(1)}, f32[128]{0:T(128)S(1)}, u32[]{:S(2)}, u32[]{:S(2)}) collective-permute-start(f32[128]{0:T(128)S(1)} %add.222), channel_id=1, source_target_pairs={{0,128},{8,136},{16,144},{24,152},{32,160},{40,168},{48,176},{56,1... | collective-permute-start | bytes 1544 | tf_op jit(solution)/shard_map/ppermute | solution.py:33
  58.0 15.6 %collective-permute-start.17 = (f32[128]{0:T(128)S(1)}, f32[128]{0:T(128)S(1)}, u32[]{:S(2)}, u32[]{:S(2)}) collective-permute-start(f32[128]{0:T(128)S(1)} %add.223), channel_id=1, source_target_pairs={{0,256},{8,264},{16,272},{24,280},{32,288},{40,296},{48,304},{56,3... | collective-permute-start | bytes 1544 | tf_op jit(solution)/shard_map/ppermute | solution.py:33
  74.6 14.3 %collective-permute-start.22 = (bf16[1,32,128]{2,1,0:T(8,128)(2,1)S(1)}, bf16[1,32,128]{2,1,0:T(8,128)(2,1)S(1)}, u32[]{:S(2)}, u32[]{:S(2)}) collective-permute-start(bf16[1,32,128]{2,1,0:T(8,128)(2,1)S(1)} %fusion.2), channel_id=1, source_target_pairs={{0,256},{8,264},{16,272},{24,280},{32,288},{40,296},{48,304},{56,3... | collective-permute-start | bytes 24584 | tf_op jit(solution)/shard_map/ppermute | solution.py:50
  88.9 9.5 %collective-permute-start.23 = (bf16[2,32,128]{2,1,0:T(8,128)(2,1)S(1)}, bf16[2,32,128]{2,1,0:T(8,128)(2,1)S(1)}, u32[]{:S(2)}, u32[]{:S(2)}) collective-permute-start(bf16[2,32,128]{2,1,0:T(8,128)(2,1)S(1)} %maximum_select_fusion.10), channel_id=1, source_target_pairs={{0,128},{8,136},{16,144},{24,152},{32,160},{40,168},{48,176},{56,1... | collective-permute-start | bytes 49160 | tf_op jit(solution)/shard_map/ppermute | solution.py:50
  98.5 6.7 %collective-permute-start.24 = (bf16[4,32,128]{2,1,0:T(8,128)(2,1)S(1)}, bf16[4,32,128]{2,1,0:T(8,128)(2,1)S(1)}, u32[]{:S(2)}, u32[]{:S(2)}) collective-permute-start(bf16[4,32,128]{2,1,0:T(8,128)(2,1)S(1)} %maximum_select_fusion.8), channel_id=1, source_target_pairs={{0,64},{8,72},{16,80},{24,88},{32,96},{40,104},{48,112},{56,120},{... | collective-permute-start | bytes 98312 | tf_op jit(solution)/shard_map/ppermute | solution.py:50
  111.4 8.5 %collective-permute-start.26 = (bf16[16,32,128]{2,1,0:T(8,128)(2,1)S(1)}, bf16[16,32,128]{2,1,0:T(8,128)(2,1)S(1)}, u32[]{:S(2)}, u32[]{:S(2)}) collective-permute-start(bf16[16,32,128]{2,1,0:T(8,128)(2,1)S(1)} %maximum_select_fusion.4), channel_id=1, source_target_pairs={{0,16},{8,24},{16,0},{24,8},{32,48},{40,56},{48,32},{56,40},{64,80... | collective-permute-start | bytes 393224 | tf_op jit(solution)/shard_map/ppermute | solution.py:50
  119.9 8.3 %collective-permute-start.27 = (bf16[32,32,128]{2,1,0:T(8,128)(2,1)S(1)}, bf16[32,32,128]{2,1,0:T(8,128)(2,1)S(1)}, u32[]{:S(2)}, u32[]{:S(2)}) collective-permute-start(bf16[32,32,128]{2,1,0:T(8,128)(2,1)S(1)} %maximum_select_fusion.2), channel_id=1, source_target_pairs={{0,8},{8,0},{16,24},{24,16},{32,40},{40,32},{48,56},{56,48},{64,72... | collective-permute-start | bytes 786440 | tf_op jit(solution)/shard_map/ppermute | solution.py:50
  129.1 238.1 %all-gather.5.cloned.1.call-start = ((), (), s32[]{:S(2)}) async-start(), calls=%async_computation.1 | async-start | bytes 4718592 | tf_op jit(solution)/shard_map/all_gather | solution.py:55
  130.9 12.0 %collective-permute-start.18 = (f32[128,128]{1,0:T(8,128)S(1)}, f32[128,128]{1,0:T(8,128)S(1)}, u32[]{:S(2)}, u32[]{:S(2)}) collective-permute-start(f32[128,128]{1,0:T(8,128)S(1)} %get-tuple-element.64), channel_id=1, source_target_pairs={{0,8},{8,16},{16,24},{24,32},{32,40},{40,48},{48,56},{56,64},{64,7... | collective-permute-start | bytes 196616 | tf_op jit(solution)/shard_map/ppermute | solution.py:15
  134.4 8.5 %collective-permute-start.20 = (f32[128,128]{1,0:T(8,128)S(1)}, f32[128,128]{1,0:T(8,128)S(1)}, u32[]{:S(2)}, u32[]{:S(2)}) collective-permute-start(f32[128,128]{1,0:T(8,128)S(1)} %get-tuple-element.65), channel_id=1, source_target_pairs={{0,1},{1,2},{2,3},{3,4},{4,5},{5,6},{6,7},{8,9},{9,10},{10,11},{11... | collective-permute-start | bytes 196616 | tf_op jit(solution)/shard_map/ppermute | solution.py:15
  135.7 7.2 %collective-permute-start.19 = (f32[128,128]{1,0:T(8,128)S(1)}, f32[128,128]{1,0:T(8,128)S(1)}, u32[]{:S(2)}, u32[]{:S(2)}) collective-permute-start(f32[128,128]{1,0:T(8,128)S(1)} %get-tuple-element.66), channel_id=1, source_target_pairs={{8,0},{16,8},{24,16},{32,24},{40,32},{48,40},{56,48},{64,56},{72,6... | collective-permute-start | bytes 196616 | tf_op jit(solution)/shard_map/ppermute | solution.py:15
  194.6 9.1 %collective-permute-start.28 = (bf16[128,128]{1,0:T(8,128)(2,1)S(1)}, bf16[128,128]{1,0:T(8,128)(2,1)S(1)}, u32[]{:S(2)}, u32[]{:S(2)}) collective-permute-start(bf16[128,128]{1,0:T(8,128)(2,1)S(1)} %get-tuple-element.72), channel_id=1, source_target_pairs={{0,8},{8,16},{16,24},{24,32},{32,40},{40,48},{48,56},{56,64},{64,7... | collective-permute-start | bytes 98312 | tf_op jit(solution)/shard_map/ppermute | solution.py:15
  228.5 7.0 %collective-permute-start.33 = (f32[3,128]{1,0:T(4,128)S(1)}, f32[3,128]{1,0:T(4,128)S(1)}, u32[]{:S(2)}, u32[]{:S(2)}) collective-permute-start(f32[3,128]{1,0:T(4,128)S(1)} %add.237), channel_id=1, source_target_pairs={{0,16},{8,24},{16,0},{24,8},{32,48},{40,56},{48,32},{56,40},{64,80... | collective-permute-start | bytes 4616 | tf_op jit(solution)/shard_map/ppermute | solution.py:33
  241.1 6.5 %collective-permute-start.35 = (f32[3,128]{1,0:T(4,128)S(1)}, f32[3,128]{1,0:T(4,128)S(1)}, u32[]{:S(2)}, u32[]{:S(2)}) collective-permute-start(f32[3,128]{1,0:T(4,128)S(1)} %add.239), channel_id=1, source_target_pairs={{0,64},{8,72},{16,80},{24,88},{32,96},{40,104},{48,112},{56,120},{... | collective-permute-start | bytes 4616 | tf_op jit(solution)/shard_map/ppermute | solution.py:33
  247.6 10.8 %collective-permute-start.36 = (f32[3,128]{1,0:T(4,128)S(1)}, f32[3,128]{1,0:T(4,128)S(1)}, u32[]{:S(2)}, u32[]{:S(2)}) collective-permute-start(f32[3,128]{1,0:T(4,128)S(1)} %add.240), channel_id=1, source_target_pairs={{0,128},{8,136},{16,144},{24,152},{32,160},{40,168},{48,176},{56,1... | collective-permute-start | bytes 4616 | tf_op jit(solution)/shard_map/ppermute | solution.py:33
  258.3 14.5 %collective-permute-start.37 = (f32[3,128]{1,0:T(4,128)S(1)}, f32[3,128]{1,0:T(4,128)S(1)}, u32[]{:S(2)}, u32[]{:S(2)}) collective-permute-start(f32[3,128]{1,0:T(4,128)S(1)} %add.241), channel_id=1, source_target_pairs={{0,256},{8,264},{16,272},{24,280},{32,288},{40,296},{48,304},{56,3... | collective-permute-start | bytes 4616 | tf_op jit(solution)/shard_map/ppermute | solution.py:33
  274.4 14.3 %collective-permute-start.42 = (bf16[1,32,128]{2,1,0:T(8,128)(2,1)S(1)}, bf16[1,32,128]{2,1,0:T(8,128)(2,1)S(1)}, u32[]{:S(2)}, u32[]{:S(2)}) collective-permute-start(bf16[1,32,128]{2,1,0:T(8,128)(2,1)S(1)} %fusion.3), channel_id=1, source_target_pairs={{0,256},{8,264},{16,272},{24,280},{32,288},{40,296},{48,304},{56,3... | collective-permute-start | bytes 24584 | tf_op jit(solution)/shard_map/ppermute | solution.py:50
  288.6 9.5 %collective-permute-start.43 = (bf16[2,32,128]{2,1,0:T(8,128)(2,1)S(1)}, bf16[2,32,128]{2,1,0:T(8,128)(2,1)S(1)}, u32[]{:S(2)}, u32[]{:S(2)}) collective-permute-start(bf16[2,32,128]{2,1,0:T(8,128)(2,1)S(1)} %maximum_select_fusion.11), channel_id=1, source_target_pairs={{0,128},{8,136},{16,144},{24,152},{32,160},{40,168},{48,176},{56,1... | collective-permute-start | bytes 49160 | tf_op jit(solution)/shard_map/ppermute | solution.py:50
  298.2 6.7 %collective-permute-start.44 = (bf16[4,32,128]{2,1,0:T(8,128)(2,1)S(1)}, bf16[4,32,128]{2,1,0:T(8,128)(2,1)S(1)}, u32[]{:S(2)}, u32[]{:S(2)}) collective-permute-start(bf16[4,32,128]{2,1,0:T(8,128)(2,1)S(1)} %maximum_select_fusion.9), channel_id=1, source_target_pairs={{0,64},{8,72},{16,80},{24,88},{32,96},{40,104},{48,112},{56,120},{... | collective-permute-start | bytes 98312 | tf_op jit(solution)/shard_map/ppermute | solution.py:50
  311.1 8.4 %collective-permute-start.46 = (bf16[16,32,128]{2,1,0:T(8,128)(2,1)S(1)}, bf16[16,32,128]{2,1,0:T(8,128)(2,1)S(1)}, u32[]{:S(2)}, u32[]{:S(2)}) collective-permute-start(bf16[16,32,128]{2,1,0:T(8,128)(2,1)S(1)} %maximum_select_fusion.5), channel_id=1, source_target_pairs={{0,16},{8,24},{16,0},{24,8},{32,48},{40,56},{48,32},{56,40},{64,80... | collective-permute-start | bytes 393224 | tf_op jit(solution)/shard_map/ppermute | solution.py:50
  319.5 8.3 %collective-permute-start.47 = (bf16[32,32,128]{2,1,0:T(8,128)(2,1)S(1)}, bf16[32,32,128]{2,1,0:T(8,128)(2,1)S(1)}, u32[]{:S(2)}, u32[]{:S(2)}) collective-permute-start(bf16[32,32,128]{2,1,0:T(8,128)(2,1)S(1)} %maximum_select_fusion.3), channel_id=1, source_target_pairs={{0,8},{8,0},{16,24},{24,16},{32,40},{40,32},{48,56},{56,48},{64,72... | collective-permute-start | bytes 786440 | tf_op jit(solution)/shard_map/ppermute | solution.py:50
  329.7 8.6 %collective-permute-start.38 = (f32[128,128]{1,0:T(8,128)S(1)}, f32[128,128]{1,0:T(8,128)S(1)}, u32[]{:S(2)}, u32[]{:S(2)}) collective-permute-start(f32[128,128]{1,0:T(8,128)S(1)} %get-tuple-element.60), channel_id=1, source_target_pairs={{0,8},{8,16},{16,24},{24,32},{32,40},{40,48},{48,56},{56,64},{64,7... | collective-permute-start | bytes 196616 | tf_op jit(solution)/shard_map/ppermute | solution.py:15
  331.9 6.5 %collective-permute-start.40 = (f32[128,128]{1,0:T(8,128)S(1)}, f32[128,128]{1,0:T(8,128)S(1)}, u32[]{:S(2)}, u32[]{:S(2)}) collective-permute-start(f32[128,128]{1,0:T(8,128)S(1)} %get-tuple-element.61), channel_id=1, source_target_pairs={{0,1},{1,2},{2,3},{3,4},{4,5},{5,6},{6,7},{8,9},{9,10},{10,11},{11... | collective-permute-start | bytes 196616 | tf_op jit(solution)/shard_map/ppermute | solution.py:15
  393.7 9.0 %collective-permute-start.48 = (bf16[128,128]{1,0:T(8,128)(2,1)S(1)}, bf16[128,128]{1,0:T(8,128)(2,1)S(1)}, u32[]{:S(2)}, u32[]{:S(2)}) collective-permute-start(bf16[128,128]{1,0:T(8,128)(2,1)S(1)} %get-tuple-element.68), channel_id=1, source_target_pairs={{0,8},{8,16},{16,24},{24,32},{32,40},{40,48},{48,56},{56,64},{64,7... | collective-permute-start | bytes 98312 | tf_op jit(solution)/shard_map/ppermute | solution.py:15
  427.6 7.0 %collective-permute-start.53 = (f32[6,128]{1,0:T(8,128)S(1)}, f32[6,128]{1,0:T(8,128)S(1)}, u32[]{:S(2)}, u32[]{:S(2)}) collective-permute-start(f32[6,128]{1,0:T(8,128)S(1)} %add.247), channel_id=1, source_target_pairs={{0,16},{8,24},{16,0},{24,8},{32,48},{40,56},{48,32},{56,40},{64,80... | collective-permute-start | bytes 9224 | tf_op jit(solution)/shard_map/ppermute | solution.py:33
  440.2 6.5 %collective-permute-start.55 = (f32[6,128]{1,0:T(8,128)S(1)}, f32[6,128]{1,0:T(8,128)S(1)}, u32[]{:S(2)}, u32[]{:S(2)}) collective-permute-start(f32[6,128]{1,0:T(8,128)S(1)} %add.249), channel_id=1, source_target_pairs={{0,64},{8,72},{16,80},{24,88},{32,96},{40,104},{48,112},{56,120},{... | collective-permute-start | bytes 9224 | tf_op jit(solution)/shard_map/ppermute | solution.py:33
  446.7 10.8 %collective-permute-start.56 = (f32[6,128]{1,0:T(8,128)S(1)}, f32[6,128]{1,0:T(8,128)S(1)}, u32[]{:S(2)}, u32[]{:S(2)}) collective-permute-start(f32[6,128]{1,0:T(8,128)S(1)} %add.250), channel_id=1, source_target_pairs={{0,128},{8,136},{16,144},{24,152},{32,160},{40,168},{48,176},{56,1... | collective-permute-start | bytes 9224 | tf_op jit(solution)/shard_map/ppermute | solution.py:33
  457.5 14.6 %collective-permute-start.57 = (f32[6,128]{1,0:T(8,128)S(1)}, f32[6,128]{1,0:T(8,128)S(1)}, u32[]{:S(2)}, u32[]{:S(2)}) collective-permute-start(f32[6,128]{1,0:T(8,128)S(1)} %add.251), channel_id=1, source_target_pairs={{0,256},{8,264},{16,272},{24,280},{32,288},{40,296},{48,304},{56,3... | collective-permute-start | bytes 9224 | tf_op jit(solution)/shard_map/ppermute | solution.py:33
  (25 other events, 741.4 us)
Sparse Core Ops, SparseCore 0:
  129.2 38.8 all-gather.2
  328.8 38.3 all-gather.4
where the time goes:
time: 484 us; the launch traced here: 482 us
  starting transfers between devices  210 us (43%)
  waiting for transfers between devices  139 us (29%)
  blocking collectives  43.9 us (9%)
  local copies, waits for them, and re-layouts  39 us (8%)
  matrix products  22.4 us (5%)
  between operations  16.4 us (3%)
  other arithmetic  10.6 us (2%)
    ppermute x18, starting transfers between devices, allsum(): lax.ppermute(value, axis, [(i, i ^ step) for i in range(count)])  110 us
    ppermute x12, starting transfers between devices, doubling_gather(): got = lax.ppermute(held, axis, [(i, i ^ step) for i in range(count)])  65.1 us
    all_gather x2, waiting for transfers between devices, doubling_gather(): lax.all_gather(held.reshape(-1, block.shape[-1]), 'gy', axis=0, tiled=True)  51.6 us
    psum x3, blocking collectives, allsum(): value = lax.psum(value, 'gy')  43.9 us
    ppermute x12, waiting for transfers between devices, doubling_gather(): got = lax.ppermute(held, axis, [(i, i ^ step) for i in range(count)])  41.3 us
    ppermute x18, waiting for transfers between devices, allsum(): lax.ppermute(value, axis, [(i, i ^ step) for i in range(count)])  40.5 us
    ppermute x16, starting transfers between devices, neighbours(): return (lax.ppermute(rows[1], axis, up), lax.ppermute(rows[0], axis, down))  35 us
    reshape x2, local copies, waits for them, and re-layouts, precondition(): placed.reshape(-1, system_count)  14.9 us
  transfers between devices with their start and end apart: 48, of which 36 were waited for; matrix products, arithmetic and copies ran while one was open for 1% of the time, Pallas kernels for 0%

commit v1 on v0

--- a/solution.py
+++ b/solution.py
@@ -6,6 +6,12 @@
 
 EPSILON = 1e-06
 KEPT_SHARE = 1.0 / 64
+
+
+def joints_resolve(unit, bus_axis):
+    high = jnp.concatenate([unit for _ in range(lax.psum(1, axis_name=bus_axis))], axis=0)
+    base_arr = lax.all_to_all(high, axis_name=bus_axis, split_axis=0, concat_axis=0, tiled=True)
+    return base_arr
 
 
 def neighbours(rows, axis):
@@ -52,7 +58,7 @@
         held = jnp.where(
             upper, jnp.concatenate([got, held], axis=0), jnp.concatenate([held, got], axis=0)
         )
-    return lax.all_gather(held.reshape(-1, block.shape[-1]), "gy", axis=0, tiled=True)
+    return joints_resolve(held.reshape(-1, block.shape[-1]), "gy")
 
 
 def gathered_order(rounds, count_y):

time: 484 us -> 508 us (1.050)
  the two profiles are of different devices: /device:TPU:8 before, /device:TPU:384 now
where the time goes in v1:
time: 508 us; the launch traced here: 506 us
  waiting for transfers between devices  243 us (48%)
  starting transfers between devices  145 us (29%)
  local copies, waits for them, and re-layouts  44 us (9%)
  blocking collectives  39.4 us (8%)
  matrix products  22.4 us (4%)
  other arithmetic  8.34 us (2%)
    ppermute x18, waiting for transfers between devices, allsum(): lax.ppermute(value, axis, [(i, i ^ step) for i in range(count)])  91.6 us
    ppermute x12, waiting for transfers between devices, doubling_gather(): got = lax.ppermute(held, axis, [(i, i ^ step) for i in range(count)])  68.5 us
    all_to_all x2, waiting for transfers between devices, joints_resolve(): lax.all_to_all(high, axis_name=bus_axis, split_axis=0, concat_axis=0, til...  61 us
    ppermute x18, starting transfers between devices, allsum(): lax.ppermute(value, axis, [(i, i ^ step) for i in range(count)])  51.8 us
    ppermute x16, starting transfers between devices, neighbours(): return (lax.ppermute(rows[1], axis, up), lax.ppermute(rows[0], axis, down))  46 us
    psum x3, blocking collectives, allsum(): value = lax.psum(value, 'gy')  39.4 us
    ppermute x12, starting transfers between devices, doubling_gather(): got = lax.ppermute(held, axis, [(i, i ^ step) for i in range(count)])  38.3 us
    ppermute x16, waiting for transfers between devices, neighbours(): return (lax.ppermute(rows[1], axis, up), lax.ppermute(rows[0], axis, down))  22.3 us
  transfers between devices with their start and end apart: 48, of which 37 were waited for; matrix products, arithmetic and copies ran while one was open for 1% of the time, Pallas kernels for 0%

profile of v1, /device:TPU:384, one launch (start us, length us, event | category | flops | bytes accessed | tf_op | source)
XLA Modules:
  0.0 506.0 jit_solution(656187828637317244)
XLA Ops:
  1.6 14.6 %psum.35 = f32[128]{0:T(128)S(1)} all-reduce(f32[128]{0:T(128)S(1)} %multiply_reduce_fusion.10), channel_id=1, replica_groups=mesh['gx'=64,'gy'=8] {'gy'}, use_global_device_ids=true, to_apply=%region_1.0 | all-reduce | flops 128 | bytes 1024 | tf_op jit(solution)/shard_map/psum | solution.py:31
  21.7 5.1 %collective-permute-start.13 = (f32[128]{0:T(128)S(1)}, f32[128]{0:T(128)S(1)}, u32[]{:S(2)}, u32[]{:S(2)}) collective-permute-start(f32[128]{0:T(128)S(1)} %add.219), channel_id=1, source_target_pairs={{0,16},{8,24},{16,0},{24,8},{32,48},{40,56},{48,32},{56,40},{64,80... | collective-permute-start | bytes 1544 | tf_op jit(solution)/shard_map/ppermute | solution.py:39
  40.4 5.4 %collective-permute-start.16 = (f32[128]{0:T(128)S(1)}, f32[128]{0:T(128)S(1)}, u32[]{:S(2)}, u32[]{:S(2)}) collective-permute-start(f32[128]{0:T(128)S(1)} %add.222), channel_id=1, source_target_pairs={{0,128},{8,136},{16,144},{24,152},{32,160},{40,168},{48,176},{56,1... | collective-permute-start | bytes 1544 | tf_op jit(solution)/shard_map/ppermute | solution.py:39
  53.8 10.2 %collective-permute-done.17 = f32[128]{0:T(128)S(1)} collective-permute-done((f32[128]{0:T(128)S(1)}, f32[128]{0:T(128)S(1)}, u32[]{:S(2)}, u32[]{:S(2)}) %collective-permute-start.17) | collective-permute-done | bytes 544 | tf_op jit(solution)/shard_map/ppermute | solution.py:39
  69.0 10.2 %collective-permute-done.22 = bf16[1,32,128]{2,1,0:T(8,128)(2,1)S(1)} collective-permute-done((bf16[1,32,128]{2,1,0:T(8,128)(2,1)S(1)}, bf16[1,32,128]{2,1,0:T(8,128)(2,1)S(1)}, u32[]{:S(2)}, u32[]{:S(2)}) %collective-permute-start.22) | collective-permute-done | bytes 8224 | tf_op jit(solution)/shard_map/ppermute | solution.py:56
  79.2 5.4 %collective-permute-start.23 = (bf16[2,32,128]{2,1,0:T(8,128)(2,1)S(1)}, bf16[2,32,128]{2,1,0:T(8,128)(2,1)S(1)}, u32[]{:S(2)}, u32[]{:S(2)}) collective-permute-start(bf16[2,32,128]{2,1,0:T(8,128)(2,1)S(1)} %maximum_select_fusion.10), channel_id=1, source_target_pairs={{0,128},{8,136},{16,144},{24,152},{32,160},{40,168},{48,176},{56,1... | collective-permute-start | bytes 49160 | tf_op jit(solution)/shard_map/ppermute | solution.py:56
  101.7 5.1 %collective-permute-start.26 = (bf16[16,32,128]{2,1,0:T(8,128)(2,1)S(1)}, bf16[16,32,128]{2,1,0:T(8,128)(2,1)S(1)}, u32[]{:S(2)}, u32[]{:S(2)}) collective-permute-start(bf16[16,32,128]{2,1,0:T(8,128)(2,1)S(1)} %maximum_select_fusion.4), channel_id=1, source_target_pairs={{0,16},{8,24},{16,0},{24,8},{32,48},{40,56},{48,32},{56,40},{64,80... | collective-permute-start | bytes 393224 | tf_op jit(solution)/shard_map/ppermute | solution.py:56
  131.2 6.6 %collective-permute-start.19 = (f32[128,128]{1,0:T(8,128)S(1)}, f32[128,128]{1,0:T(8,128)S(1)}, u32[]{:S(2)}, u32[]{:S(2)}) collective-permute-start(f32[128,128]{1,0:T(8,128)S(1)} %get-tuple-element.66), channel_id=1, source_target_pairs={{8,0},{16,8},{24,16},{32,24},{40,32},{48,40},{56,48},{64,56},{72,6... | collective-permute-start | bytes 196616 | tf_op jit(solution)/shard_map/ppermute | solution.py:21
  148.0 28.0 %all-to-all-done = bf16[8,2048,128]{2,1,0:T(8,128)(2,1)} async-done(((bf16[8,2048,128]{2,1,0:T(8,128)(2,1)}), bf16[8,2048,128]{2,1,0:T(8,128)(2,1)}, u32[]{:S(2)}, u32[]{:S(2)}) %all-to-all-start) | async-done | bytes 4194336 | tf_op jit(solution)/shard_map/all_to_all | solution.py:13
  175.9 7.4 %reshape.138 = bf16[512,4096]{1,0:T(8,128)(2,1)} reshape(bf16[8,2048,128]{2,1,0:T(8,128)(2,1)} %all-to-all-done) | data formatting | bytes 8388608 | tf_op jit(solution)/shard_map/reshape | solution.py:130
  183.3 6.6 %convolution_convert_fusion.1 = bf16[512,4096]{1,0:T(8,128)(2,1)} fusion(bf16[512,4096]{1,0:T(8,128)(2,1)} %reshape.138, s32[512]{0:T(512)S(1)} %gather_fusion.1), kind=kOutput, calls=%fused_computation.10 | convolution fusion | flops 2149842944 | bytes 8390656 | tf_op jit(solution)/shard_map/dot_general | solution.py:131
  189.9 7.5 %reshape.139 = bf16[16384,128]{1,0:T(8,128)(2,1)} reshape(bf16[512,4096]{1,0:T(8,128)(2,1)} %convolution_convert_fusion.1) | data formatting | bytes 8388608 | tf_op jit(solution)/shard_map/reshape | solution.py:135
  206.8 6.6 %collective-permute-start.29 = (bf16[128,128]{1,0:T(8,128)(2,1)S(1)}, bf16[128,128]{1,0:T(8,128)(2,1)S(1)}, u32[]{:S(2)}, u32[]{:S(2)}) collective-permute-start(bf16[128,128]{1,0:T(8,128)(2,1)S(1)} %get-tuple-element.74), channel_id=1, source_target_pairs={{8,0},{16,8},{24,16},{32,24},{40,32},{48,40},{56,48},{64,56},{72,6... | collective-permute-start | bytes 98312 | tf_op jit(solution)/shard_map/ppermute | solution.py:21
  215.4 7.2 %collective-permute-done.28 = bf16[128,128]{1,0:T(8,128)(2,1)S(1)} collective-permute-done((bf16[128,128]{1,0:T(8,128)(2,1)S(1)}, bf16[128,128]{1,0:T(8,128)(2,1)S(1)}, u32[]{:S(2)}, u32[]{:S(2)}) %collective-permute-start.28) | collective-permute-done | bytes 32800 | tf_op jit(solution)/shard_map/ppermute | solution.py:21
  225.2 12.4 %psum.36 = f32[3,128]{1,0:T(4,128)S(1)} all-reduce(f32[3,128]{1,0:T(4,128)S(1)} %pad_maximum_fusion.4), channel_id=1, replica_groups=mesh['gx'=64,'gy'=8] {'gy'}, use_global_device_ids=true, to_apply=%region_6.7 | all-reduce | flops 384 | bytes 3072 | tf_op jit(solution)/shard_map/psum | solution.py:31
  245.0 5.1 collective-permute-done.33
  265.6 5.7 %collective-permute-done.36 = f32[3,128]{1,0:T(4,128)S(1)} collective-permute-done((f32[3,128]{1,0:T(4,128)S(1)}, f32[3,128]{1,0:T(4,128)S(1)}, u32[]{:S(2)}, u32[]{:S(2)}) %collective-permute-start.36) | collective-permute-done | bytes 1568 | tf_op jit(solution)/shard_map/ppermute | solution.py:39
  274.1 11.4 %collective-permute-done.37 = f32[3,128]{1,0:T(4,128)S(1)} collective-permute-done((f32[3,128]{1,0:T(4,128)S(1)}, f32[3,128]{1,0:T(4,128)S(1)}, u32[]{:S(2)}, u32[]{:S(2)}) %collective-permute-start.37) | collective-permute-done | bytes 1568 | tf_op jit(solution)/shard_map/ppermute | solution.py:39
  289.8 11.8 %collective-permute-done.42 = bf16[1,32,128]{2,1,0:T(8,128)(2,1)S(1)} collective-permute-done((bf16[1,32,128]{2,1,0:T(8,128)(2,1)S(1)}, bf16[1,32,128]{2,1,0:T(8,128)(2,1)S(1)}, u32[]{:S(2)}, u32[]{:S(2)}) %collective-permute-start.42) | collective-permute-done | bytes 8224 | tf_op jit(solution)/shard_map/ppermute | solution.py:56
  304.9 6.4 %collective-permute-done.43 = bf16[2,32,128]{2,1,0:T(8,128)(2,1)S(1)} collective-permute-done((bf16[2,32,128]{2,1,0:T(8,128)(2,1)S(1)}, bf16[2,32,128]{2,1,0:T(8,128)(2,1)S(1)}, u32[]{:S(2)}, u32[]{:S(2)}) %collective-permute-start.43) | collective-permute-done | bytes 16416 | tf_op jit(solution)/shard_map/ppermute | solution.py:56
  326.1 6.4 %collective-permute-done.46 = bf16[16,32,128]{2,1,0:T(8,128)(2,1)S(1)} collective-permute-done((bf16[16,32,128]{2,1,0:T(8,128)(2,1)S(1)}, bf16[16,32,128]{2,1,0:T(8,128)(2,1)S(1)}, u32[]{:S(2)}, u32[]{:S(2)}) %collective-permute-start.46) | collective-permute-done | bytes 131104 | tf_op jit(solution)/shard_map/ppermute | solution.py:56
  334.7 6.2 %collective-permute-done.47 = bf16[32,32,128]{2,1,0:T(8,128)(2,1)S(1)} collective-permute-done((bf16[32,32,128]{2,1,0:T(8,128)(2,1)S(1)}, bf16[32,32,128]{2,1,0:T(8,128)(2,1)S(1)}, u32[]{:S(2)}, u32[]{:S(2)}) %collective-permute-start.47) | collective-permute-done | bytes 262176 | tf_op jit(solution)/shard_map/ppermute | solution.py:56
  359.7 5.2 %collective-permute-done.38 = f32[128,128]{1,0:T(8,128)S(1)} collective-permute-done((f32[128,128]{1,0:T(8,128)S(1)}, f32[128,128]{1,0:T(8,128)S(1)}, u32[]{:S(2)}, u32[]{:S(2)}) %collective-permute-start.38) | collective-permute-done | bytes 65568 | tf_op jit(solution)/shard_map/ppermute | solution.py:21
  365.3 33.0 %all-to-all-done.1 = bf16[8,2048,128]{2,1,0:T(8,128)(2,1)} async-done(((bf16[8,2048,128]{2,1,0:T(8,128)(2,1)}), bf16[8,2048,128]{2,1,0:T(8,128)(2,1)}, u32[]{:S(2)}, u32[]{:S(2)}) %all-to-all-start.1) | async-done | bytes 4194336 | tf_op jit(solution)/shard_map/all_to_all | solution.py:13
  398.3 7.4 %reshape.141 = bf16[512,4096]{1,0:T(8,128)(2,1)} reshape(bf16[8,2048,128]{2,1,0:T(8,128)(2,1)} %all-to-all-done.1) | data formatting | bytes 8388608 | tf_op jit(solution)/shard_map/reshape | solution.py:130
  405.7 6.6 %convolution_convert_fusion = bf16[512,4096]{1,0:T(8,128)(2,1)} fusion(bf16[512,4096]{1,0:T(8,128)(2,1)} %reshape.141, s32[512]{0:T(512)S(1)} %gather_fusion.1), kind=kOutput, calls=%fused_computation.9 | convolution fusion | flops 2149842944 | bytes 8390656 | tf_op jit(solution)/shard_map/dot_general | solution.py:131
  412.3 7.4 %reshape.142 = bf16[16384,128]{1,0:T(8,128)(2,1)} reshape(bf16[512,4096]{1,0:T(8,128)(2,1)} %convolution_convert_fusion) | data formatting | bytes 8388608 | tf_op jit(solution)/shard_map/reshape | solution.py:135
  435.0 5.2 %collective-permute-done.48 = bf16[128,128]{1,0:T(8,128)(2,1)S(1)} collective-permute-done((bf16[128,128]{1,0:T(8,128)(2,1)S(1)}, bf16[128,128]{1,0:T(8,128)(2,1)S(1)}, u32[]{:S(2)}, u32[]{:S(2)}) %collective-permute-start.48) | collective-permute-done | bytes 32800 | tf_op jit(solution)/shard_map/ppermute | solution.py:21
  442.8 12.4 %psum.37 = f32[6,128]{1,0:T(8,128)S(1)} all-reduce(f32[6,128]{1,0:T(8,128)S(1)} %stack.126), channel_id=1, replica_groups=mesh['gx'=64,'gy'=8] {'gy'}, use_global_device_ids=true, to_apply=%region_18.19 | all-reduce | flops 768 | bytes 6144 | tf_op jit(solution)/shard_map/psum | solution.py:31
  462.7 5.1 %collective-permute-done.53 = f32[6,128]{1,0:T(8,128)S(1)} collective-permute-done((f32[6,128]{1,0:T(8,128)S(1)}, f32[6,128]{1,0:T(8,128)S(1)}, u32[]{:S(2)}, u32[]{:S(2)}) %collective-permute-start.53) | collective-permute-done | bytes 3104 | tf_op jit(solution)/shard_map/ppermute | solution.py:39
  483.1 5.9 %collective-permute-done.56 = f32[6,128]{1,0:T(8,128)S(1)} collective-permute-done((f32[6,128]{1,0:T(8,128)S(1)}, f32[6,128]{1,0:T(8,128)S(1)}, u32[]{:S(2)}, u32[]{:S(2)}) %collective-permute-start.56) | collective-permute-done | bytes 3104 | tf_op jit(solution)/shard_map/ppermute | solution.py:39
  491.4 11.8 %collective-permute-done.57 = f32[6,128]{1,0:T(8,128)S(1)} collective-permute-done((f32[6,128]{1,0:T(8,128)S(1)}, f32[6,128]{1,0:T(8,128)S(1)}, u32[]{:S(2)}, u32[]{:S(2)}) %collective-permute-start.57) | collective-permute-done | bytes 3104 | tf_op jit(solution)/shard_map/ppermute | solution.py:39
  (191 shorter events, 211.7 us)
Async XLA Ops:
  40.4 9.4 %collective-permute-start.16 = (f32[128]{0:T(128)S(1)}, f32[128]{0:T(128)S(1)}, u32[]{:S(2)}, u32[]{:S(2)}) collective-permute-start(f32[128]{0:T(128)S(1)} %add.222), channel_id=1, source_target_pairs={{0,128},{8,136},{16,144},{24,152},{32,160},{40,168},{48,176},{56,1... | collective-permute-start | bytes 1544 | tf_op jit(solution)/shard_map/ppermute | solution.py:39
  49.8 14.2 %collective-permute-start.17 = (f32[128]{0:T(128)S(1)}, f32[128]{0:T(128)S(1)}, u32[]{:S(2)}, u32[]{:S(2)}) collective-permute-start(f32[128]{0:T(128)S(1)} %add.223), channel_id=1, source_target_pairs={{0,256},{8,264},{16,272},{24,280},{32,288},{40,296},{48,304},{56,3... | collective-permute-start | bytes 1544 | tf_op jit(solution)/shard_map/ppermute | solution.py:39
  65.0 14.3 %collective-permute-start.22 = (bf16[1,32,128]{2,1,0:T(8,128)(2,1)S(1)}, bf16[1,32,128]{2,1,0:T(8,128)(2,1)S(1)}, u32[]{:S(2)}, u32[]{:S(2)}) collective-permute-start(bf16[1,32,128]{2,1,0:T(8,128)(2,1)S(1)} %fusion.2), channel_id=1, source_target_pairs={{0,256},{8,264},{16,272},{24,280},{32,288},{40,296},{48,304},{56,3... | collective-permute-start | bytes 24584 | tf_op jit(solution)/shard_map/ppermute | solution.py:56
  79.2 9.5 %collective-permute-start.23 = (bf16[2,32,128]{2,1,0:T(8,128)(2,1)S(1)}, bf16[2,32,128]{2,1,0:T(8,128)(2,1)S(1)}, u32[]{:S(2)}, u32[]{:S(2)}) collective-permute-start(bf16[2,32,128]{2,1,0:T(8,128)(2,1)S(1)} %maximum_select_fusion.10), channel_id=1, source_target_pairs={{0,128},{8,136},{16,144},{24,152},{32,160},{40,168},{48,176},{56,1... | collective-permute-start | bytes 49160 | tf_op jit(solution)/shard_map/ppermute | solution.py:56
  101.7 8.4 %collective-permute-start.26 = (bf16[16,32,128]{2,1,0:T(8,128)(2,1)S(1)}, bf16[16,32,128]{2,1,0:T(8,128)(2,1)S(1)}, u32[]{:S(2)}, u32[]{:S(2)}) collective-permute-start(bf16[16,32,128]{2,1,0:T(8,128)(2,1)S(1)} %maximum_select_fusion.4), channel_id=1, source_target_pairs={{0,16},{8,24},{16,0},{24,8},{32,48},{40,56},{48,32},{56,40},{64,80... | collective-permute-start | bytes 393224 | tf_op jit(solution)/shard_map/ppermute | solution.py:56
  110.0 8.3 %collective-permute-start.27 = (bf16[32,32,128]{2,1,0:T(8,128)(2,1)S(1)}, bf16[32,32,128]{2,1,0:T(8,128)(2,1)S(1)}, u32[]{:S(2)}, u32[]{:S(2)}) collective-permute-start(bf16[32,32,128]{2,1,0:T(8,128)(2,1)S(1)} %maximum_select_fusion.2), channel_id=1, source_target_pairs={{0,8},{8,0},{16,24},{24,16},{32,40},{40,32},{48,56},{56,48},{64,72... | collective-permute-start | bytes 786440 | tf_op jit(solution)/shard_map/ppermute | solution.py:56
  121.0 54.9 %all-to-all-start = ((bf16[8,2048,128]{2,1,0:T(8,128)(2,1)}), bf16[8,2048,128]{2,1,0:T(8,128)(2,1)}, u32[]{:S(2)}, u32[]{:S(2)}) async-start(bf16[8,2048,128]{2,1,0:T(8,128)(2,1)} %bitcast.207), calls=%async_computation | async-start | bytes 8388608 | tf_op jit(solution)/shard_map/all_to_all | solution.py:13
  126.9 16.4 %collective-permute-start.21 = (f32[128,128]{1,0:T(8,128)S(1)}, f32[128,128]{1,0:T(8,128)S(1)}, u32[]{:S(2)}, u32[]{:S(2)}) collective-permute-start(f32[128,128]{1,0:T(8,128)S(1)} %get-tuple-element.67), channel_id=1, source_target_pairs={{1,0},{2,1},{3,2},{4,3},{5,4},{6,5},{7,6},{9,8},{10,9},{11,10},{12... | collective-permute-start | bytes 196616 | tf_op jit(solution)/shard_map/ppermute | solution.py:21
  128.2 15.1 %collective-permute-start.20 = (f32[128,128]{1,0:T(8,128)S(1)}, f32[128,128]{1,0:T(8,128)S(1)}, u32[]{:S(2)}, u32[]{:S(2)}) collective-permute-start(f32[128,128]{1,0:T(8,128)S(1)} %get-tuple-element.65), channel_id=1, source_target_pairs={{0,1},{1,2},{2,3},{3,4},{4,5},{5,6},{6,7},{8,9},{9,10},{10,11},{11... | collective-permute-start | bytes 196616 | tf_op jit(solution)/shard_map/ppermute | solution.py:21
  131.2 12.1 %collective-permute-start.19 = (f32[128,128]{1,0:T(8,128)S(1)}, f32[128,128]{1,0:T(8,128)S(1)}, u32[]{:S(2)}, u32[]{:S(2)}) collective-permute-start(f32[128,128]{1,0:T(8,128)S(1)} %get-tuple-element.66), channel_id=1, source_target_pairs={{8,0},{16,8},{24,16},{32,24},{40,32},{48,40},{56,48},{64,56},{72,6... | collective-permute-start | bytes 196616 | tf_op jit(solution)/shard_map/ppermute | solution.py:21
  137.8 9.8 %collective-permute-start.18 = (f32[128,128]{1,0:T(8,128)S(1)}, f32[128,128]{1,0:T(8,128)S(1)}, u32[]{:S(2)}, u32[]{:S(2)}) collective-permute-start(f32[128,128]{1,0:T(8,128)S(1)} %get-tuple-element.64), channel_id=1, source_target_pairs={{0,8},{8,16},{16,24},{24,32},{32,40},{40,48},{48,56},{56,64},{64,7... | collective-permute-start | bytes 196616 | tf_op jit(solution)/shard_map/ppermute | solution.py:21
  202.5 12.9 %collective-permute-start.31 = (bf16[128,128]{1,0:T(8,128)(2,1)S(1)}, bf16[128,128]{1,0:T(8,128)(2,1)S(1)}, u32[]{:S(2)}, u32[]{:S(2)}) collective-permute-start(bf16[128,128]{1,0:T(8,128)(2,1)S(1)} %get-tuple-element.75), channel_id=1, source_target_pairs={{1,0},{2,1},{3,2},{4,3},{5,4},{6,5},{7,6},{9,8},{10,9},{11,10},{12... | collective-permute-start | bytes 98312 | tf_op jit(solution)/shard_map/ppermute | solution.py:21
  203.8 11.6 %collective-permute-start.30 = (bf16[128,128]{1,0:T(8,128)(2,1)S(1)}, bf16[128,128]{1,0:T(8,128)(2,1)S(1)}, u32[]{:S(2)}, u32[]{:S(2)}) collective-permute-start(bf16[128,128]{1,0:T(8,128)(2,1)S(1)} %get-tuple-element.73), channel_id=1, source_target_pairs={{0,1},{1,2},{2,3},{3,4},{4,5},{5,6},{6,7},{8,9},{9,10},{10,11},{11... | collective-permute-start | bytes 98312 | tf_op jit(solution)/shard_map/ppermute | solution.py:21
  206.8 8.6 %collective-permute-start.29 = (bf16[128,128]{1,0:T(8,128)(2,1)S(1)}, bf16[128,128]{1,0:T(8,128)(2,1)S(1)}, u32[]{:S(2)}, u32[]{:S(2)}) collective-permute-start(bf16[128,128]{1,0:T(8,128)(2,1)S(1)} %get-tuple-element.74), channel_id=1, source_target_pairs={{8,0},{16,8},{24,16},{32,24},{40,32},{48,40},{56,48},{64,56},{72,6... | collective-permute-start | bytes 98312 | tf_op jit(solution)/shard_map/ppermute | solution.py:21
  213.4 9.1 %collective-permute-start.28 = (bf16[128,128]{1,0:T(8,128)(2,1)S(1)}, bf16[128,128]{1,0:T(8,128)(2,1)S(1)}, u32[]{:S(2)}, u32[]{:S(2)}) collective-permute-start(bf16[128,128]{1,0:T(8,128)(2,1)S(1)} %get-tuple-element.72), channel_id=1, source_target_pairs={{0,8},{8,16},{16,24},{24,32},{32,40},{40,48},{48,56},{56,64},{64,7... | collective-permute-start | bytes 98312 | tf_op jit(solution)/shard_map/ppermute | solution.py:21
  243.1 7.0 %collective-permute-start.33 = (f32[3,128]{1,0:T(4,128)S(1)}, f32[3,128]{1,0:T(4,128)S(1)}, u32[]{:S(2)}, u32[]{:S(2)}) collective-permute-start(f32[3,128]{1,0:T(4,128)S(1)} %add.237), channel_id=1, source_target_pairs={{0,16},{8,24},{16,0},{24,8},{32,48},{40,56},{48,32},{56,40},{64,80... | collective-permute-start | bytes 4616 | tf_op jit(solution)/shard_map/ppermute | solution.py:39
  261.9 9.4 %collective-permute-start.36 = (f32[3,128]{1,0:T(4,128)S(1)}, f32[3,128]{1,0:T(4,128)S(1)}, u32[]{:S(2)}, u32[]{:S(2)}) collective-permute-start(f32[3,128]{1,0:T(4,128)S(1)} %add.240), channel_id=1, source_target_pairs={{0,128},{8,136},{16,144},{24,152},{32,160},{40,168},{48,176},{56,1... | collective-permute-start | bytes 4616 | tf_op jit(solution)/shard_map/ppermute | solution.py:39
  271.3 14.2 %collective-permute-start.37 = (f32[3,128]{1,0:T(4,128)S(1)}, f32[3,128]{1,0:T(4,128)S(1)}, u32[]{:S(2)}, u32[]{:S(2)}) collective-permute-start(f32[3,128]{1,0:T(4,128)S(1)} %add.241), channel_id=1, source_target_pairs={{0,256},{8,264},{16,272},{24,280},{32,288},{40,296},{48,304},{56,3... | collective-permute-start | bytes 4616 | tf_op jit(solution)/shard_map/ppermute | solution.py:39
  287.0 14.6 %collective-permute-start.42 = (bf16[1,32,128]{2,1,0:T(8,128)(2,1)S(1)}, bf16[1,32,128]{2,1,0:T(8,128)(2,1)S(1)}, u32[]{:S(2)}, u32[]{:S(2)}) collective-permute-start(bf16[1,32,128]{2,1,0:T(8,128)(2,1)S(1)} %fusion.3), channel_id=1, source_target_pairs={{0,256},{8,264},{16,272},{24,280},{32,288},{40,296},{48,304},{56,3... | collective-permute-start | bytes 24584 | tf_op jit(solution)/shard_map/ppermute | solution.py:56
  301.6 9.6 %collective-permute-start.43 = (bf16[2,32,128]{2,1,0:T(8,128)(2,1)S(1)}, bf16[2,32,128]{2,1,0:T(8,128)(2,1)S(1)}, u32[]{:S(2)}, u32[]{:S(2)}) collective-permute-start(bf16[2,32,128]{2,1,0:T(8,128)(2,1)S(1)} %maximum_select_fusion.11), channel_id=1, source_target_pairs={{0,128},{8,136},{16,144},{24,152},{32,160},{40,168},{48,176},{56,1... | collective-permute-start | bytes 49160 | tf_op jit(solution)/shard_map/ppermute | solution.py:56
  324.2 8.4 %collective-permute-start.46 = (bf16[16,32,128]{2,1,0:T(8,128)(2,1)S(1)}, bf16[16,32,128]{2,1,0:T(8,128)(2,1)S(1)}, u32[]{:S(2)}, u32[]{:S(2)}) collective-permute-start(bf16[16,32,128]{2,1,0:T(8,128)(2,1)S(1)} %maximum_select_fusion.5), channel_id=1, source_target_pairs={{0,16},{8,24},{16,0},{24,8},{32,48},{40,56},{48,32},{56,40},{64,80... | collective-permute-start | bytes 393224 | tf_op jit(solution)/shard_map/ppermute | solution.py:56
  332.6 8.3 %collective-permute-start.47 = (bf16[32,32,128]{2,1,0:T(8,128)(2,1)S(1)}, bf16[32,32,128]{2,1,0:T(8,128)(2,1)S(1)}, u32[]{:S(2)}, u32[]{:S(2)}) collective-permute-start(bf16[32,32,128]{2,1,0:T(8,128)(2,1)S(1)} %maximum_select_fusion.3), channel_id=1, source_target_pairs={{0,8},{8,0},{16,24},{24,16},{32,40},{40,32},{48,56},{56,48},{64,72... | collective-permute-start | bytes 786440 | tf_op jit(solution)/shard_map/ppermute | solution.py:56
  343.5 54.8 %all-to-all-start.1 = ((bf16[8,2048,128]{2,1,0:T(8,128)(2,1)}), bf16[8,2048,128]{2,1,0:T(8,128)(2,1)}, u32[]{:S(2)}, u32[]{:S(2)}) async-start(bf16[8,2048,128]{2,1,0:T(8,128)(2,1)} %bitcast.208), calls=%async_computation.1 | async-start | bytes 8388608 | tf_op jit(solution)/shard_map/all_to_all | solution.py:13
  349.2 10.2 %collective-permute-start.41 = (f32[128,128]{1,0:T(8,128)S(1)}, f32[128,128]{1,0:T(8,128)S(1)}, u32[]{:S(2)}, u32[]{:S(2)}) collective-permute-start(f32[128,128]{1,0:T(8,128)S(1)} %get-tuple-element.63), channel_id=1, source_target_pairs={{1,0},{2,1},{3,2},{4,3},{5,4},{6,5},{7,6},{9,8},{10,9},{11,10},{12... | collective-permute-start | bytes 196616 | tf_op jit(solution)/shard_map/ppermute | solution.py:21
  350.5 8.9 %collective-permute-start.40 = (f32[128,128]{1,0:T(8,128)S(1)}, f32[128,128]{1,0:T(8,128)S(1)}, u32[]{:S(2)}, u32[]{:S(2)}) collective-permute-start(f32[128,128]{1,0:T(8,128)S(1)} %get-tuple-element.61), channel_id=1, source_target_pairs={{0,1},{1,2},{2,3},{3,4},{4,5},{5,6},{6,7},{8,9},{9,10},{10,11},{11... | collective-permute-start | bytes 196616 | tf_op jit(solution)/shard_map/ppermute | solution.py:21
  355.4 9.5 %collective-permute-start.38 = (f32[128,128]{1,0:T(8,128)S(1)}, f32[128,128]{1,0:T(8,128)S(1)}, u32[]{:S(2)}, u32[]{:S(2)}) collective-permute-start(f32[128,128]{1,0:T(8,128)S(1)} %get-tuple-element.60), channel_id=1, source_target_pairs={{0,8},{8,16},{16,24},{24,32},{32,40},{40,48},{48,56},{56,64},{64,7... | collective-permute-start | bytes 196616 | tf_op jit(solution)/shard_map/ppermute | solution.py:21
  424.8 10.2 %collective-permute-start.51 = (bf16[128,128]{1,0:T(8,128)(2,1)S(1)}, bf16[128,128]{1,0:T(8,128)(2,1)S(1)}, u32[]{:S(2)}, u32[]{:S(2)}) collective-permute-start(bf16[128,128]{1,0:T(8,128)(2,1)S(1)} %get-tuple-element.71), channel_id=1, source_target_pairs={{1,0},{2,1},{3,2},{4,3},{5,4},{6,5},{7,6},{9,8},{10,9},{11,10},{12... | collective-permute-start | bytes 98312 | tf_op jit(solution)/shard_map/ppermute | solution.py:21
  426.1 8.9 %collective-permute-start.50 = (bf16[128,128]{1,0:T(8,128)(2,1)S(1)}, bf16[128,128]{1,0:T(8,128)(2,1)S(1)}, u32[]{:S(2)}, u32[]{:S(2)}) collective-permute-start(bf16[128,128]{1,0:T(8,128)(2,1)S(1)} %get-tuple-element.69), channel_id=1, source_target_pairs={{0,1},{1,2},{2,3},{3,4},{4,5},{5,6},{6,7},{8,9},{9,10},{10,11},{11... | collective-permute-start | bytes 98312 | tf_op jit(solution)/shard_map/ppermute | solution.py:21
  431.1 9.1 %collective-permute-start.48 = (bf16[128,128]{1,0:T(8,128)(2,1)S(1)}, bf16[128,128]{1,0:T(8,128)(2,1)S(1)}, u32[]{:S(2)}, u32[]{:S(2)}) collective-permute-start(bf16[128,128]{1,0:T(8,128)(2,1)S(1)} %get-tuple-element.68), channel_id=1, source_target_pairs={{0,8},{8,16},{16,24},{24,32},{32,40},{40,48},{48,56},{56,64},{64,7... | collective-permute-start | bytes 98312 | tf_op jit(solution)/shard_map/ppermute | solution.py:21
  460.8 7.0 %collective-permute-start.53 = (f32[6,128]{1,0:T(8,128)S(1)}, f32[6,128]{1,0:T(8,128)S(1)}, u32[]{:S(2)}, u32[]{:S(2)}) collective-permute-start(f32[6,128]{1,0:T(8,128)S(1)} %add.247), channel_id=1, source_target_pairs={{0,16},{8,24},{16,0},{24,8},{32,48},{40,56},{48,32},{56,40},{64,80... | collective-permute-start | bytes 9224 | tf_op jit(solution)/shard_map/ppermute | solution.py:39
  479.6 9.4 %collective-permute-start.56 = (f32[6,128]{1,0:T(8,128)S(1)}, f32[6,128]{1,0:T(8,128)S(1)}, u32[]{:S(2)}, u32[]{:S(2)}) collective-permute-start(f32[6,128]{1,0:T(8,128)S(1)} %add.250), channel_id=1, source_target_pairs={{0,128},{8,136},{16,144},{24,152},{32,160},{40,168},{48,176},{56,1... | collective-permute-start | bytes 9224 | tf_op jit(solution)/shard_map/ppermute | solution.py:39
  489.0 14.2 %collective-permute-start.57 = (f32[6,128]{1,0:T(8,128)S(1)}, f32[6,128]{1,0:T(8,128)S(1)}, u32[]{:S(2)}, u32[]{:S(2)}) collective-permute-start(f32[6,128]{1,0:T(8,128)S(1)} %add.251), channel_id=1, source_target_pairs={{0,256},{8,264},{16,272},{24,280},{32,288},{40,296},{48,304},{56,3... | collective-permute-start | bytes 9224 | tf_op jit(solution)/shard_map/ppermute | solution.py:39
  (27 other events, 426.7 us)
